TPU v7x, 128 devices: a whole 4x4x4 slice. The times are simulated.
128 devices in a mesh: wave: 8 (over z_lo, x), strip: 16 (over y, z_hi, core).
Axes of the slice: x: 4, y: 4, z: 4 (z_hi: 2, z_lo: 2; z = z_hi * 2 + z_lo), core: 2. Of those that a mesh axis runs over, the one named last changes fastest.
Arguments:
- unit_params: float32 [9, 16, 24576], P(None, 'strip', 'wave'), may hold values from 0 to 1
- observed: bfloat16 [4, 256, 1536, 256], P(None, 'wave', 'strip'), may hold values from -3 to 3
- psf_rows: bfloat16 [256, 4, 65], P('wave'), may hold values from -0.75 to 0.75
- psf_cols: bfloat16 [256, 4, 65], P('wave'), may hold values from -0.75 to 0.75
- pixel_mask: int32 [1536, 256], P('strip'), may hold values 0 or 1
- strip_lengths: int32 [16], P('strip'), may hold values from 32 to 96, as said below
Outputs:
- param_grad: float32 [9, 16, 24576], P(None, 'strip', 'wave')
Inputs may be any that keep to these rules, and one draw needn't show every extreme that they name: `strip_lengths`: the strip lengths sum to 1024; in every draw one strip holds 96 rows and one holds 32.
All inputs are finite; a program needn't handle non-finite values. No bound on the sum of `pixel_mask` on one device may be relied on, other than what follows from the above.
Results may differ from a plain program's by a relative error of at most 0.00098.
Values may be sent and summed in bfloat16 or wider, within the bound.
No kernel may reach another device: no remote copies, remote signals or barrier semaphores. Data moves between devices by JAX's collectives and lax.ppermute only.
A program may use at most 192 MiB of HBM per device.

v0:
```python
import jax
import jax.numpy as jnp
from jax import lax
from jax.sharding import PartitionSpec as P

parameter_low = (0.2, 0.4, 2.0, -0.8, 0.4, 0.3, 0.0, 0.0, 0.0)
parameter_span = (0.4, 0.6, 18.0, 1.6, 0.8, 1.2, 1.5, 3.141592653589793, 3.141592653589793)
stokes_weight = (1.0, 3.0, 3.0, 2.0)
loss_scale = 0.03125


def passed_along(shard, axis, by):
    count = lax.axis_size(axis)
    pairs = [(i, i + by) for i in range(count) if 0 <= i + by < count]
    return lax.ppermute(shard, axis, pairs)


def profile(distance, damping):
    scaled = distance / damping
    return 1.0 / (1.0 + scaled * scaled)


def stokes_model(unit_params, wave_grid):
    physical = [
        parameter_low[number] + parameter_span[number] * unit_params[number] for number in range(9)
    ]
    (
        source_zero,
        source_slope,
        strength,
        doppler,
        line_width,
        damping,
        zeeman_split,
        incline,
        azimuth,
    ) = physical
    offset = (wave_grid[:, None, None] - doppler) / line_width
    split_ratio = zeeman_split / line_width
    centre = profile(offset, damping)
    upper_line = profile(offset - split_ratio, damping)
    lower_line = profile(offset + split_ratio, damping)
    cosine = jnp.cos(incline)
    sine_value = jnp.sin(incline)
    sine_square = sine_value * sine_value
    absorb_total = 1.0 + strength * (
        centre * sine_square * 0.5 + (upper_line + lower_line) * (1.0 + cosine * cosine) * 0.25
    )
    linear = strength * (centre - 0.5 * (upper_line + lower_line)) * sine_square * 0.5
    linear_cosine = linear * jnp.cos(2.0 * azimuth)
    linear_sine = linear * jnp.sin(2.0 * azimuth)
    circular = strength * (lower_line - upper_line) * cosine * 0.5
    denominator = (
        absorb_total * absorb_total
        - linear_cosine * linear_cosine
        - linear_sine * linear_sine
        - circular * circular
    )
    source_ratio = source_slope / denominator
    return jnp.stack(
        [
            source_zero + source_ratio * absorb_total,
            -source_ratio * linear_cosine,
            -source_ratio * linear_sine,
            -source_ratio * circular,
        ]
    )


def band_tables(tap_table, out_rows, tap_count):
    in_rows = out_rows + tap_count - 1
    target_row = lax.broadcasted_iota(jnp.int32, (out_rows, in_rows, tap_count), 0)
    source_row = lax.broadcasted_iota(jnp.int32, (out_rows, in_rows, tap_count), 1)
    tap_index = lax.broadcasted_iota(jnp.int32, (out_rows, in_rows, tap_count), 2)
    selector = (source_row - target_row == tap_index).astype(jnp.bfloat16)
    return jnp.einsum(
        "wkt,ijt->wkij", tap_table, selector, preferred_element_type=jnp.float32
    ).astype(jnp.bfloat16)


def column_tables(tap_table, columns, tap_count):
    radius = tap_count // 2
    source_column = lax.broadcasted_iota(jnp.int32, (columns, columns, tap_count), 0)
    target_column = lax.broadcasted_iota(jnp.int32, (columns, columns, tap_count), 1)
    tap_index = lax.broadcasted_iota(jnp.int32, (columns, columns, tap_count), 2)
    selector = (source_column - target_column + radius == tap_index).astype(jnp.bfloat16)
    return jnp.einsum(
        "wkt,xyt->wkxy", tap_table, selector, preferred_element_type=jnp.float32
    ).astype(jnp.bfloat16)


def extend(upper_rim, middle, lower_rim, length, axis_index):
    radius = upper_rim.shape[axis_index]
    widened = jnp.concatenate([upper_rim, middle, jnp.zeros_like(upper_rim)], axis=axis_index)
    return lax.dynamic_update_slice_in_dim(widened, lower_rim, radius + length, axis_index)


def per_device(unit_params, observed, psf_rows, psf_cols, pixel_mask, strip_lengths):
    stokes_count, wave_count, capacity, columns = observed.shape
    tap_count = psf_rows.shape[2]
    radius = tap_count // 2
    gathered = lax.all_gather(unit_params, "wave", axis=2, tiled=True)
    own_params = gathered.reshape(gathered.shape[0], capacity, columns)
    length = strip_lengths[0]
    wave_pos = lax.axis_index("wave")
    levels = (wave_pos * wave_count + jnp.arange(wave_count, dtype=jnp.int32)).astype(jnp.float32)
    wave_grid = -3.0 + 6.0 * levels / (wave_count * lax.axis_size("wave") - 1)
    row_index = jnp.arange(capacity, dtype=jnp.int32)
    rows_live = (row_index < length).astype(jnp.float32)
    model_own = (stokes_model(own_params, wave_grid) * rows_live[:, None]).astype(jnp.bfloat16)
    tail_rows = lax.dynamic_slice_in_dim(model_own, length - radius, radius, 2)
    upper_rim = passed_along(tail_rows, "strip", 1)
    lower_rim = passed_along(model_own[:, :, :radius], "strip", -1)
    model_wide = extend(upper_rim, model_own, lower_rim, length, 2)
    row_band = band_tables(psf_rows, capacity, tap_count)
    column_band = column_tables(psf_cols, columns, tap_count)
    live_mask = pixel_mask.astype(jnp.float32) * rows_live[:, None]
    weight_square = jnp.array(stokes_weight, jnp.float32)
    weight_square = weight_square * weight_square
    block_size = 4
    block_count = wave_count // block_size

    def forward(number, residual_all):
        first_wave = number * block_size
        model_block = lax.dynamic_slice_in_dim(model_wide, first_wave, block_size, 1)
        band_block = lax.dynamic_slice_in_dim(row_band, first_wave, block_size, 0)
        column_block = lax.dynamic_slice_in_dim(column_band, first_wave, block_size, 0)
        observed_block = lax.dynamic_slice_in_dim(observed, first_wave, block_size, 1)
        row_pass = jnp.einsum(
            "wkij,swjc->kswic", band_block, model_block, preferred_element_type=jnp.float32
        ).astype(jnp.bfloat16)
        blurred = jnp.einsum(
            "kswic,wkcd->swid", row_pass, column_block, preferred_element_type=jnp.float32
        )
        residual = (
            loss_scale
            * weight_square[:, None, None, None]
            * live_mask
            * (blurred - observed_block.astype(jnp.float32))
        ).astype(jnp.bfloat16)
        return lax.dynamic_update_slice_in_dim(residual_all, residual, first_wave, 1)

    residual_all = lax.fori_loop(0, block_count, forward, jnp.zeros(observed.shape, jnp.bfloat16))
    row_back = band_tables(psf_rows[:, :, ::-1], capacity, tap_count)
    tail_residual = lax.dynamic_slice_in_dim(residual_all, length - radius, radius, 2)
    upper_resid = passed_along(tail_residual, "strip", 1)
    lower_resid = passed_along(residual_all[:, :, :radius], "strip", -1)
    residual_wide = extend(upper_resid, residual_all, lower_resid, length, 2)

    def backward(number, gradient_sum):
        first_wave = number * block_size
        residual_block = lax.dynamic_slice_in_dim(residual_wide, first_wave, block_size, 1)
        column_block = lax.dynamic_slice_in_dim(column_band, first_wave, block_size, 0)
        back_block = lax.dynamic_slice_in_dim(row_back, first_wave, block_size, 0)
        grid_block = lax.dynamic_slice_in_dim(wave_grid, first_wave, block_size, 0)
        across = jnp.einsum(
            "swjc,wkdc->kswjd", residual_block, column_block, preferred_element_type=jnp.float32
        ).astype(jnp.bfloat16)
        adjoint = (
            jnp.einsum("wkij,kswjc->swic", back_block, across, preferred_element_type=jnp.float32)
            * rows_live[:, None]
        )

        def model_of(params_now):
            return stokes_model(params_now, grid_block)

        unused_model, pullback = jax.vjp(model_of, own_params)
        return gradient_sum + pullback(adjoint)[0]

    gradient_local = lax.fori_loop(
        0, block_count, backward, jnp.zeros(own_params.shape, jnp.float32)
    )
    gradient_flat = gradient_local.reshape(gathered.shape)
    gradient_total = lax.psum(gradient_flat, "wave")
    share_width = unit_params.shape[2]
    return lax.dynamic_slice_in_dim(gradient_total, wave_pos * share_width, share_width, 2)


def solution(mesh):
    return jax.shard_map(
        per_device,
        mesh=mesh,
        in_specs=(
            P(None, "strip", "wave"),
            P(None, "wave", "strip", None),
            P("wave", None, None),
            P("wave", None, None),
            P("strip", None),
            P("strip"),
        ),
        out_specs=P(None, "strip", "wave"),
        check_vma=False,
    )
```

profile of v0, /device:TPU:0, one launch (start us, length us, event | category | flops | bytes accessed | tf_op | source)
XLA Modules:
  0.0 510.9 jit_solution(6636742498582574275)
XLA Ops:
  6.5 31.1 %all_gather.3 = f32[9,1,24576]{2,1,0:T(1,128)S(1)} all-gather(f32[9,1,3072]{2,1,0:T(1,128)} %param.11), channel_id=1, replica_groups=mesh['wave'=8,'strip'=16] {'wave'}, dimensions={2}, use_global_device_ids=true | all-gather | bytes 995328 | tf_op jit(solution)/shard_map/all_gather | solution.py:102
  37.6 9.9 %fusion.103 = (f32[24576]{0:T(1024)S(1)}, f32[24576]{0:T(1024)S(1)}, f32[24576]{0:T(1024)S(1)}, f32[24576]{0:T(1024)S(1)}, f32[24576]{0:T(1024)S(1)}, /*index=5*...) fusion(f32[9,1,24576]{2,1,0:T(1,128)S(1)} %all_gather.3), kind=kLoop, calls=%fused_computation.198 | loop fusion | flops 442368 | bytes 1966080 | tf_op jit(solution)/shard_map/add | solution.py:25
  48.7 5.3 %multiply_add_fusion.8 = (f32[1,32,96,256]{3,2,1,0:T(8,128)S(1)}, f32[1,32,96,256]{3,2,1,0:T(8,128)S(1)}, f32[1,32,96,256]{3,2,1,0:T(8,128)S(1)}, f32[1,32,96,256]{3,2,1,0:T(8,128)S(1)}) fusion(f32[96,256]{1,0:T(8,128)S(1)} %get-tuple-element.546, f32[96,256]{1,0:T(8,128)S(1)} %add.585, f32[96,256]{1,0:T(8,128)S(1)} %get-tuple-element.545, ...), kind=kLoop, calls=%fused_computation.166 | loop fusion | flops 37748736 | bytes 13860992 | tf_op jit(solution)/shard_map/add | solution.py:62
  64.1 8.5 %convert_bitcast_fusion = bf16[32,4,256,256]{3,0,1,2:T(8,128)(2,1)} fusion(bf16[32,4,65]{2,1,0:T(4,128)(2,1)S(1)} %copy-done.4), kind=kOutput, calls=%fused_computation.149 | convolution fusion | flops 1111687168 | bytes 16793856 | tf_op jit(solution)/shard_map/wkt,xyt->wkxy/dot_general | solution.py:87
  72.6 16.3 %copy.20 = bf16[32,4,256,256]{3,2,1,0:T(8,128)(2,1)} copy(bf16[32,4,256,256]{3,0,1,2:T(8,128)(2,1)} %convert_bitcast_fusion) | data formatting | bytes 33554432
  92.9 10.1 %maximum_maximum_fusion = bf16[4,32,160,256]{3,2,1,0:T(8,128)(2,1)} fusion(bf16[4,32,96,256]{3,2,1,0:T(8,128)(2,1)} %copy-done.1, bf16[4,32,32,256]{3,2,1,0:T(8,128)(2,1)} %collective-permute-done, bf16[160]{0:T(256)(128)(2,1)S(1)} %pad.113.clone), kind=kLoop, calls=%fused_computation.152 | loop fusion | flops 31457280 | bytes 18874688 | tf_op jit(solution)/shard_map/concatenate | solution.py:94
  103.0 20.4 %dynamic_update_slice.13 = bf16[4,32,160,256]{3,2,1,0:T(8,128)(2,1)} dynamic-update-slice(bf16[4,32,160,256]{3,2,1,0:T(8,128)(2,1)} %maximum_maximum_fusion, bf16[4,32,32,256]{3,2,1,0:T(8,128)(2,1)} %collective-permute-done.1, s32[]{:T(128)} %constant.278.clone.1, s32[]{:T(128)} %constant.278.clone.1, s32[]{:T(128)S(6)} %select_n.37, s32[]{:T(128)} %constant.278.clone.1) | dynamic-update-slice | bytes 4194308 | tf_op jit(solution)/shard_map/dynamic_update_slice | solution.py:95
  126.7 58.5 %while.31 = (s32[]{:T(128)}, bf16[4,32,96,256]{3,2,1,0:T(8,128)(2,1)}, f32[96,256]{1,0:T(8,128)S(1)}, bf16[32,4,256,256]{3,2,1,0:T(8,128)(2,1)}, bf16[4,32,160,2...) while((s32[]{:T(128)}, ...), condition=%wide.region_1.0_spmd.clone, body=%wide.region_0.0_spmd.clone.sunk | while | flops 1311866880 | bytes 9897691 | solution.py:143
  173.0 4.0 fusion.130
  185.2 5.4 %fusion.112 = (bf16[4,32,32,256]{3,2,1,0:T(8,128)(2,1)}, bf16[4,32,32,256]{3,2,1,0:T(8,128)(2,1)}) fusion(bf16[4,32,96,256]{3,2,1,0:T(8,128)(2,1)} %get-tuple-element.364, s32[]{:T(128)S(6)} %select_n.36), kind=kLoop, calls=%fused_computation.217 | loop fusion | bytes 8388612 | tf_op jit(solution)/shard_map/slice | solution.py:147
  190.6 22.0 %collective-permute-start.2 = (bf16[4,32,32,256]{3,2,1,0:T(8,128)(2,1)}, bf16[4,32,32,256]{3,2,1,0:T(8,128)(2,1)}, u32[]{:S(2)}, u32[]{:S(2)}) collective-permute-start(bf16[4,32,32,256]{3,2,1,0:T(8,128)(2,1)} %get-tuple-element.537), channel_id=1, source_target_pairs={{0,1},{1,2},{2,3},{3,4},{4,5},{5,6},{6,7},{7,8},{8,9},{9,10},{10,1... | collective-permute-start | bytes 6291464 | tf_op jit(solution)/shard_map/ppermute | solution.py:15
  219.7 4.0 convert_bitcast_fusion.1
  223.7 7.9 %maximum_maximum_fusion.1 = bf16[4,32,160,256]{3,2,1,0:T(8,128)(2,1)} fusion(bf16[4,32,96,256]{3,2,1,0:T(8,128)(2,1)S(1)} %copy-done, bf16[4,32,32,256]{3,2,1,0:T(8,128)(2,1)} %collective-permute-done.2, bf16[160]{0:T(256)(128)(2,1)S(1)} %pad.113.clone), kind=kLoop, calls=%fused_computation.153 | loop fusion | flops 31457280 | bytes 18874688 | tf_op jit(solution)/shard_map/concatenate | solution.py:94
  231.6 20.4 %dynamic_update_slice.14 = bf16[4,32,160,256]{3,2,1,0:T(8,128)(2,1)} dynamic-update-slice(bf16[4,32,160,256]{3,2,1,0:T(8,128)(2,1)} %maximum_maximum_fusion.1, bf16[4,32,32,256]{3,2,1,0:T(8,128)(2,1)} %collective-permute-done.3, s32[]{:T(128)} %constant.278.clone.1, s32[]{:T(128)} %constant.278.clone.1, s32[]{:T(128)S(6)} %select_n.37, s32[]{:T(128)} %constant.278.clone.1) | dynamic-update-slice | bytes 4194308 | tf_op jit(solution)/shard_map/dynamic_update_slice | solution.py:95
  252.0 134.8 %while.32 = (s32[]{:T(128)}, f32[9,96,256]{2,1,0:T(8,128)S(1)}, f32[9,96,256]{2,1,0:T(8,128)S(1)}, f32[32]{0:T(128)S(1)}, bf16[32,4,256,256]{3,2,1,0:T(8,128)(2,...) while((s32[]{:T(128)}, f32[9,96,256]{2,1,0:T(8,128)S(1)}, ...), condition=%wide.region_21.22_spmd.clone, body=%wide.region_2.21_spmd.clone.sunk | while | flops 1872642304 | bytes 34342920 | solution.py:170
  255.2 4.9 fusion.134
  272.0 4.9 fusion.134
  288.9 4.9 fusion.134
  305.7 4.9 fusion.134
  322.6 4.9 fusion.134
  339.4 4.9 fusion.134
  356.3 4.9 fusion.134
  373.1 4.9 fusion.134
  388.6 113.9 %all-reduce.11.cloned.1.call-done = f32[9,1,24576]{2,1,0:T(1,128)} async-done(((f32[9,1,24576]{2,1,0:T(1,128)}), f32[9,1,24576]{2,1,0:T(1,128)}) %all-reduce.11.cloned.1.call-update) | async-done | bytes 884752 | tf_op jit(solution)/shard_map/psum | solution.py:174
  (216 shorter events, 177.7 us)
Async XLA Ops:
  6.5 496.0 %all-reduce.11.cloned.1.call-start = ((), (), s32[]{:S(2)}) async-start(), calls=%async_computation | async-start | bytes 1769472 | tf_op jit(solution)/shard_map/psum | solution.py:174
  56.1 3.9 copy-start.1
  56.1 8.0 %copy-start.4 = (bf16[32,4,65]{2,1,0:T(4,128)(2,1)S(1)}, bf16[32,4,65]{2,1,0:T(4,128)(2,1)}, u32[]{:S(2)}) copy-start(bf16[32,4,65]{2,1,0:T(4,128)(2,1)} %param.14) | copy-start | bytes 49924
  60.0 32.9 %collective-permute-start = (bf16[4,32,32,256]{3,2,1,0:T(8,128)(2,1)}, bf16[4,32,32,256]{3,2,1,0:T(8,128)(2,1)}, u32[]{:S(2)}, u32[]{:S(2)}) collective-permute-start(bf16[4,32,32,256]{3,2,1,0:T(8,128)(2,1)} %get-tuple-element.539), channel_id=1, source_target_pairs={{0,1},{1,2},{2,3},{3,4},{4,5},{5,6},{6,7},{7,8},{8,9},{9,10},{10,1... | collective-permute-start | bytes 6291464 | tf_op jit(solution)/shard_map/ppermute | solution.py:15
  62.6 40.3 %collective-permute-start.1 = (bf16[4,32,32,256]{3,2,1,0:T(8,128)(2,1)}, bf16[4,32,32,256]{3,2,1,0:T(8,128)(2,1)}, u32[]{:S(2)}, u32[]{:S(2)}) collective-permute-start(bf16[4,32,32,256]{3,2,1,0:T(8,128)(2,1)} %get-tuple-element.538), channel_id=1, source_target_pairs={{1,0},{2,1},{3,2},{4,3},{5,4},{6,5},{7,6},{8,7},{9,8},{10,9},{11,1... | collective-permute-start | bytes 6291464 | tf_op jit(solution)/shard_map/ppermute | solution.py:15
  72.6 16.4 %copy-start.3 = (s32[96,256]{1,0:T(8,128)S(1)}, s32[96,256]{1,0:T(8,128)}, u32[]{:S(2)}) copy-start(s32[96,256]{1,0:T(8,128)} %param.15) | copy-start | bytes 294916
  72.6 16.4 %copy-start.2 = (bf16[32,4,65]{2,1,0:T(4,128)(2,1)S(1)}, bf16[32,4,65]{2,1,0:T(4,128)(2,1)}, u32[]{:S(2)}) copy-start(bf16[32,4,65]{2,1,0:T(4,128)(2,1)} %param.13) | copy-start | bytes 49924
  123.3 3.4 copy-start.5
  190.6 33.1 %collective-permute-start.2 = (bf16[4,32,32,256]{3,2,1,0:T(8,128)(2,1)}, bf16[4,32,32,256]{3,2,1,0:T(8,128)(2,1)}, u32[]{:S(2)}, u32[]{:S(2)}) collective-permute-start(bf16[4,32,32,256]{3,2,1,0:T(8,128)(2,1)} %get-tuple-element.537), channel_id=1, source_target_pairs={{0,1},{1,2},{2,3},{3,4},{4,5},{5,6},{6,7},{7,8},{8,9},{9,10},{10,1... | collective-permute-start | bytes 6291464 | tf_op jit(solution)/shard_map/ppermute | solution.py:15
  212.6 19.0 %collective-permute-start.3 = (bf16[4,32,32,256]{3,2,1,0:T(8,128)(2,1)}, bf16[4,32,32,256]{3,2,1,0:T(8,128)(2,1)}, u32[]{:S(2)}, u32[]{:S(2)}) collective-permute-start(bf16[4,32,32,256]{3,2,1,0:T(8,128)(2,1)} %get-tuple-element.536), channel_id=1, source_target_pairs={{1,0},{2,1},{3,2},{4,3},{5,4},{6,5},{7,6},{8,7},{9,8},{10,9},{11,1... | collective-permute-start | bytes 6291464 | tf_op jit(solution)/shard_map/ppermute | solution.py:15
  219.7 4.0 copy-start
Sparse Core Ops, SparseCore 0:
  388.8 113.6 all-reduce.10
where the time goes:
time: 514 us; the launch traced here: 511 us
  local copies, waits for them, and re-layouts  122 us (24%)
  other arithmetic  114 us (22%)
  waiting for transfers between devices  114 us (22%)
  matrix products  87 us (17%)
  blocking collectives  31.1 us (6%)
  starting transfers between devices  27.5 us (5%)
  between operations  14.3 us (3%)
    psum x1, waiting for transfers between devices, per_device(): gradient_total = lax.psum(gradient_flat, 'wave')  114 us
    dynamic_update_slice x2, local copies, waits for them, and re-layouts, extend(): lax.dynamic_update_slice_in_dim(widened, lower_rim, radius + length, axis...  40.8 us
    dot_general x8, matrix products, backward(): jnp.einsum('wkij,kswjc->swic', back_block, across, preferred_element_type...  39.1 us
    dot_general x8, matrix products, forward(): jnp.einsum('kswic,wkcd->swid', row_pass, column_block, preferred_element_...  31.6 us
    all_gather x1, blocking collectives, per_device(): gathered = lax.all_gather(unit_params, 'wave', axis=2, tiled=True)  31.1 us
    ppermute x4, starting transfers between devices, passed_along(): return lax.ppermute(shard, axis, pairs)  27.5 us
    mul x32, other arithmetic, stokes_model(): parameter_span[number] * unit_params[number]  22.7 us
    dynamic_slice x8, local copies, waits for them, and re-layouts, backward(): back_block = lax.dynamic_slice_in_dim(row_back, first_wave, block_size, 0)  20.2 us
  transfers between devices with their start and end apart: 5, of which 1 were waited for; matrix products, arithmetic and copies ran while one was open for 11% of the time, Pallas kernels for 0%

commit v1 on v0

--- a/solution.py
+++ b/solution.py
@@ -171,7 +171,7 @@
         0, block_count, backward, jnp.zeros(own_params.shape, jnp.float32)
     )
     gradient_flat = gradient_local.reshape(gathered.shape)
-    gradient_total = lax.psum(gradient_flat, "wave")
+    gradient_total = jnp.sum(lax.all_gather(gradient_flat, "wave"), axis=0)
     share_width = unit_params.shape[2]
     return lax.dynamic_slice_in_dim(gradient_total, wave_pos * share_width, share_width, 2)
 

time: 514 us -> 531 us (1.033)
  other arithmetic: 114 us -> 133 us
  local copies, waits for them, and re-layouts: 122 us -> 107 us
  matrix products: 87 us -> 94.7 us
  waiting for transfers between devices: 114 us -> 120 us
    all_gather x0 -> x1, waiting for transfers between devices: none -> 120 us  [per_device(): gradient_total = jnp.sum(lax.all_gather(gradient_flat, 'wave'), axis=0)]
    psum x1 -> x0, waiting for transfers between devices: 114 us -> none  [per_device(): gradient_total = lax.psum(gradient_flat, 'wave')]
    reduce_sum x0 -> x1, other arithmetic: none -> 19.7 us  [per_device(): gradient_total = jnp.sum(lax.all_gather(gradient_flat, 'wave'), axis=0)]
    dot_general x8, matrix products: 31.6 us -> 39.3 us  [forward(): jnp.einsum('kswic,wkcd->swid', row_pass, column_block, preferred_element_...]
    dynamic_update_slice x8 -> x0, local copies, waits for them, and re-layouts: 7.64 us -> none  [forward(): lax.dynamic_update_slice_in_dim(residual_all, residual, first_wave, 1)]
    dynamic_slice x16 -> x8, local copies, waits for them, and re-layouts: 18.2 us -> 13.3 us  [forward(): band_block = lax.dynamic_slice_in_dim(row_band, first_wave, block_size, 0)]
  transfers between devices with their start and end apart: 5 -> 5, of which waited for: 1 -> 1; matrix products, arithmetic and copies ran while one was open for 11% -> 10% of each run, Pallas kernels for 0% -> 0%
where the time goes in v1:
time: 531 us; the launch traced here: 528 us
  other arithmetic  133 us (25%)
  waiting for transfers between devices  120 us (23%)
  local copies, waits for them, and re-layouts  107 us (20%)
  matrix products  94.7 us (18%)
  blocking collectives  31.1 us (6%)
  starting transfers between devices  27.4 us (5%)
  between operations  14.3 us (3%)
    all_gather x1, waiting for transfers between devices, per_device(): gradient_total = jnp.sum(lax.all_gather(gradient_flat, 'wave'), axis=0)  120 us
    dynamic_update_slice x2, local copies, waits for them, and re-layouts, extend(): lax.dynamic_update_slice_in_dim(widened, lower_rim, radius + length, axis...  40.4 us
    dot_general x8, matrix products, forward(): jnp.einsum('kswic,wkcd->swid', row_pass, column_block, preferred_element_...  39.3 us
    dot_general x8, matrix products, backward(): jnp.einsum('wkij,kswjc->swic', back_block, across, preferred_element_type...  39 us
    all_gather x1, blocking collectives, per_device(): gathered = lax.all_gather(unit_params, 'wave', axis=2, tiled=True)  31.1 us
    ppermute x4, starting transfers between devices, passed_along(): return lax.ppermute(shard, axis, pairs)  27.3 us
    mul x32, other arithmetic, stokes_model(): parameter_span[number] * unit_params[number]  22.7 us
    dynamic_slice x8, local copies, waits for them, and re-layouts, backward(): back_block = lax.dynamic_slice_in_dim(row_back, first_wave, block_size, 0)  20.2 us
  transfers between devices with their start and end apart: 5, of which 1 were waited for; matrix products, arithmetic and copies ran while one was open for 10% of the time, Pallas kernels for 0%

profile of v1, /device:TPU:0, one launch (start us, length us, event | category | flops | bytes accessed | tf_op | source)
XLA Modules:
  0.0 527.6 jit_solution(13017271283852919784)
XLA Ops:
  6.5 31.1 %all_gather.6 = f32[9,1,24576]{2,1,0:T(1,128)S(1)} all-gather(f32[9,1,3072]{2,1,0:T(1,128)} %param.11), channel_id=1, replica_groups=mesh['wave'=8,'strip'=16] {'wave'}, dimensions={2}, use_global_device_ids=true | all-gather | bytes 995328 | tf_op jit(solution)/shard_map/all_gather | solution.py:102
  37.6 9.9 %fusion.111 = (f32[24576]{0:T(1024)S(1)}, f32[24576]{0:T(1024)S(1)}, f32[24576]{0:T(1024)S(1)}, f32[24576]{0:T(1024)S(1)}, f32[24576]{0:T(1024)S(1)}, /*index=5*...) fusion(f32[9,1,24576]{2,1,0:T(1,128)S(1)} %all_gather.6), kind=kLoop, calls=%fused_computation.198 | loop fusion | flops 442368 | bytes 1966080 | tf_op jit(solution)/shard_map/add | solution.py:25
  48.7 5.3 %multiply_add_fusion.8 = (f32[1,32,96,256]{3,2,0,1:T(8,128)S(1)}, f32[1,32,96,256]{3,2,0,1:T(8,128)S(1)}, f32[1,32,96,256]{3,2,0,1:T(8,128)S(1)}, f32[1,32,96,256]{3,2,0,1:T(8,128)S(1)}) fusion(f32[96,256]{1,0:T(8,128)S(1)} %get-tuple-element.576, f32[96,256]{1,0:T(8,128)S(1)} %add.583, f32[96,256]{1,0:T(8,128)S(1)} %get-tuple-element.575, ...), kind=kLoop, calls=%fused_computation.166 | loop fusion | flops 37748736 | bytes 13860992 | tf_op jit(solution)/shard_map/add | solution.py:62
  64.1 8.5 %convert_bitcast_fusion = bf16[32,4,256,256]{3,0,1,2:T(8,128)(2,1)} fusion(bf16[32,4,65]{2,1,0:T(4,128)(2,1)S(1)} %copy-done.4), kind=kOutput, calls=%fused_computation.149 | convolution fusion | flops 1111687168 | bytes 16793856 | tf_op jit(solution)/shard_map/wkt,xyt->wkxy/dot_general | solution.py:87
  72.6 16.3 %copy.45 = bf16[32,4,256,256]{3,2,1,0:T(8,128)(2,1)} copy(bf16[32,4,256,256]{3,0,1,2:T(8,128)(2,1)} %convert_bitcast_fusion) | data formatting | bytes 33554432
  92.9 10.1 %maximum_maximum_fusion = bf16[4,32,160,256]{3,2,0,1:T(8,128)(2,1)} fusion(bf16[4,32,96,256]{3,2,0,1:T(8,128)(2,1)} %copy-done.1, bf16[4,32,32,256]{3,2,0,1:T(8,128)(2,1)} %collective-permute-done, bf16[160]{0:T(256)(128)(2,1)S(1)} %pad.113.clone), kind=kLoop, calls=%fused_computation.152 | loop fusion | flops 31457280 | bytes 18874688 | tf_op jit(solution)/shard_map/concatenate | solution.py:94
  103.0 20.2 %dynamic_update_slice.13 = bf16[4,32,160,256]{3,2,0,1:T(8,128)(2,1)} dynamic-update-slice(bf16[4,32,160,256]{3,2,0,1:T(8,128)(2,1)} %maximum_maximum_fusion, bf16[4,32,32,256]{3,2,0,1:T(8,128)(2,1)} %collective-permute-done.1, s32[]{:T(128)} %constant.279.clone.1, s32[]{:T(128)} %constant.279.clone.1, s32[]{:T(128)S(6)} %select_n.37, s32[]{:T(128)} %constant.279.clone.1) | dynamic-update-slice | bytes 4194308 | tf_op jit(solution)/shard_map/dynamic_update_slice | solution.py:95
  126.6 53.5 %while.31 = (s32[]{:T(128)}, bf16[4,32,96,256]{3,2,0,1:T(8,128)(2,1)}, f32[96,256]{1,0:T(8,128)S(1)}, bf16[32,4,256,256]{3,2,1,0:T(8,128)(2,1)}, bf16[4,32,160,2...) while((s32[]{:T(128)}, ...), condition=%wide.region_1.0_spmd.clone, body=%wide.region_0.0_spmd.clone.sunk | while | flops 1311866880 | bytes 7342295 | solution.py:143
  128.4 4.9 fusion.136
  135.1 4.9 fusion.136
  141.7 4.9 fusion.136
  148.4 5.0 fusion.136
  155.1 4.9 fusion.136
  161.8 4.9 fusion.136
  168.5 4.9 fusion.136
  175.2 4.9 fusion.136
  180.1 5.5 %fusion.120 = (bf16[4,32,32,256]{3,2,0,1:T(8,128)(2,1)}, bf16[4,32,32,256]{3,2,0,1:T(8,128)(2,1)}) fusion(bf16[4,32,96,256]{3,2,0,1:T(8,128)(2,1)} %get-tuple-element.364, s32[]{:T(128)S(6)} %select_n.36), kind=kLoop, calls=%fused_computation.217 | loop fusion | bytes 8388612 | tf_op jit(solution)/shard_map/slice | solution.py:147
  185.6 22.0 %collective-permute-start.2 = (bf16[4,32,32,256]{3,2,0,1:T(8,128)(2,1)}, bf16[4,32,32,256]{3,2,0,1:T(8,128)(2,1)}, u32[]{:S(2)}, u32[]{:S(2)}) collective-permute-start(bf16[4,32,32,256]{3,2,0,1:T(8,128)(2,1)} %get-tuple-element.567), channel_id=1, source_target_pairs={{0,1},{1,2},{2,3},{3,4},{4,5},{5,6},{6,7},{7,8},{8,9},{9,10},{10,1... | collective-permute-start | bytes 6291464 | tf_op jit(solution)/shard_map/ppermute | solution.py:15
  215.7 8.3 %maximum_maximum_fusion.1 = bf16[4,32,160,256]{3,2,0,1:T(8,128)(2,1)} fusion(bf16[4,32,96,256]{3,2,0,1:T(8,128)(2,1)S(1)} %copy-done, bf16[4,32,32,256]{3,2,0,1:T(8,128)(2,1)} %collective-permute-done.2, bf16[160]{0:T(256)(128)(2,1)S(1)} %pad.113.clone), kind=kLoop, calls=%fused_computation.153 | loop fusion | flops 31457280 | bytes 18874688 | tf_op jit(solution)/shard_map/concatenate | solution.py:94
  224.0 20.2 %dynamic_update_slice.14 = bf16[4,32,160,256]{3,2,0,1:T(8,128)(2,1)} dynamic-update-slice(bf16[4,32,160,256]{3,2,0,1:T(8,128)(2,1)} %maximum_maximum_fusion.1, bf16[4,32,32,256]{3,2,0,1:T(8,128)(2,1)} %collective-permute-done.3, s32[]{:T(128)} %constant.279.clone.1, s32[]{:T(128)} %constant.279.clone.1, s32[]{:T(128)S(6)} %select_n.37, s32[]{:T(128)} %constant.279.clone.1) | dynamic-update-slice | bytes 4194308 | tf_op jit(solution)/shard_map/dynamic_update_slice | solution.py:95
  244.2 134.8 %while.32 = (s32[]{:T(128)}, f32[9,96,256]{2,1,0:T(8,128)S(1)}, f32[9,96,256]{2,1,0:T(8,128)S(1)}, f32[32]{0:T(128)S(1)}, bf16[32,4,256,256]{3,2,1,0:T(8,128)(2,...) while((s32[]{:T(128)}, f32[9,96,256]{2,1,0:T(8,128)S(1)}, ...), condition=%wide.region_21.22_spmd.clone, body=%wide.region_2.21_spmd.clone.sunk | while | flops 1872642304 | bytes 34342920 | solution.py:170
  264.2 4.9 fusion.140
  380.8 119.5 %all-gather.2.cloned.1.call-done = f32[8,9,1,24576]{3,2,1,0:T(1,128)} async-done(((f32[1,9,1,24576]{3,2,1,0:T(1,128)}), f32[8,9,1,24576]{3,2,1,0:T(1,128)}) %all-gather.2.cloned.1.call-update) | async-done | bytes 7077904 | tf_op jit(solution)/shard_map/all_gather | solution.py:174
  500.3 19.7 %reduce_sum.423 = f32[9,24576]{1,0:T(8,128)S(1)} reduce(f32[8,9,1,24576]{3,2,1,0:T(1,128)} %all-gather.2.cloned.1.call-done, f32[]{:T(128)} %constant.280.clone.1), dimensions={0,2}, to_apply=%region_22.23 | reduce | flops 1548288 | bytes 7962628 | tf_op jit(solution)/shard_map/reduce_sum | solution.py:174
  (202 shorter events, 171.7 us)
Async XLA Ops:
  6.5 493.8 %all-gather.2.cloned.1.call-start = ((), (), s32[]{:S(2)}) async-start(), calls=%async_computation | async-start | bytes 7962624 | tf_op jit(solution)/shard_map/all_gather | solution.py:174
  56.1 3.9 copy-start.1
  56.1 8.0 %copy-start.4 = (bf16[32,4,65]{2,1,0:T(4,128)(2,1)S(1)}, bf16[32,4,65]{2,1,0:T(4,128)(2,1)}, u32[]{:S(2)}) copy-start(bf16[32,4,65]{2,1,0:T(4,128)(2,1)} %param.14) | copy-start | bytes 49924
  60.0 32.9 %collective-permute-start = (bf16[4,32,32,256]{3,2,0,1:T(8,128)(2,1)}, bf16[4,32,32,256]{3,2,0,1:T(8,128)(2,1)}, u32[]{:S(2)}, u32[]{:S(2)}) collective-permute-start(bf16[4,32,32,256]{3,2,0,1:T(8,128)(2,1)} %get-tuple-element.569), channel_id=1, source_target_pairs={{0,1},{1,2},{2,3},{3,4},{4,5},{5,6},{6,7},{7,8},{8,9},{9,10},{10,1... | collective-permute-start | bytes 6291464 | tf_op jit(solution)/shard_map/ppermute | solution.py:15
  62.7 40.4 %collective-permute-start.1 = (bf16[4,32,32,256]{3,2,0,1:T(8,128)(2,1)}, bf16[4,32,32,256]{3,2,0,1:T(8,128)(2,1)}, u32[]{:S(2)}, u32[]{:S(2)}) collective-permute-start(bf16[4,32,32,256]{3,2,0,1:T(8,128)(2,1)} %get-tuple-element.568), channel_id=1, source_target_pairs={{1,0},{2,1},{3,2},{4,3},{5,4},{6,5},{7,6},{8,7},{9,8},{10,9},{11,1... | collective-permute-start | bytes 6291464 | tf_op jit(solution)/shard_map/ppermute | solution.py:15
  72.6 16.4 %copy-start.3 = (s32[96,256]{1,0:T(8,128)S(1)}, s32[96,256]{1,0:T(8,128)}, u32[]{:S(2)}) copy-start(s32[96,256]{1,0:T(8,128)} %param.15) | copy-start | bytes 294916
  72.6 16.4 %copy-start.2 = (bf16[32,4,65]{2,1,0:T(4,128)(2,1)S(1)}, bf16[32,4,65]{2,1,0:T(4,128)(2,1)}, u32[]{:S(2)}) copy-start(bf16[32,4,65]{2,1,0:T(4,128)(2,1)} %param.13) | copy-start | bytes 49924
  123.2 3.4 copy-start.5
  185.6 30.1 %collective-permute-start.2 = (bf16[4,32,32,256]{3,2,0,1:T(8,128)(2,1)}, bf16[4,32,32,256]{3,2,0,1:T(8,128)(2,1)}, u32[]{:S(2)}, u32[]{:S(2)}) collective-permute-start(bf16[4,32,32,256]{3,2,0,1:T(8,128)(2,1)} %get-tuple-element.567), channel_id=1, source_target_pairs={{0,1},{1,2},{2,3},{3,4},{4,5},{5,6},{6,7},{7,8},{8,9},{9,10},{10,1... | collective-permute-start | bytes 6291464 | tf_op jit(solution)/shard_map/ppermute | solution.py:15
  207.6 16.4 %collective-permute-start.3 = (bf16[4,32,32,256]{3,2,0,1:T(8,128)(2,1)}, bf16[4,32,32,256]{3,2,0,1:T(8,128)(2,1)}, u32[]{:S(2)}, u32[]{:S(2)}) collective-permute-start(bf16[4,32,32,256]{3,2,0,1:T(8,128)(2,1)} %get-tuple-element.566), channel_id=1, source_target_pairs={{1,0},{2,1},{3,2},{4,3},{5,4},{6,5},{7,6},{8,7},{9,8},{10,9},{11,1... | collective-permute-start | bytes 6291464 | tf_op jit(solution)/shard_map/ppermute | solution.py:15
  211.7 4.0 copy-start
Sparse Core Ops, SparseCore 0:
  380.9 119.3 all-gather.1
